TPU v7x, 512 devices: a whole 4x4x16 slice. The times are simulated.
512 devices in a mesh: seq: 64 (over z, x), tp: 8 (over y, core).
Axes of the slice: x: 4, y: 4, z: 16, core: 2. Of those that a mesh axis runs over, the one named last changes fastest.
Arguments:
- mamba_x: bfloat16 [4096, 8192], P('seq', 'tp'), may hold values from -6 to 6
- gate_z: bfloat16 [4096, 8192], P('seq', 'tp'), may hold values from -6 to 6
- b_in: bfloat16 [4096, 1024], P('seq', 'tp'), may hold values from -1.25 to 1.25
- c_in: bfloat16 [4096, 1024], P('seq', 'tp'), may hold values from -1.25 to 1.25
- dt_raw: float32 [128, 4096], P('tp', 'seq'), may hold values from -2 to 24576
- a_log: float32 [128], P('tp'), may hold values from -14 to -3
- skip_d: float32 [128], P('tp'), may hold values from 0.5 to 1.5
- norm_gain: float32 [8192], P('tp'), may hold values from 0.5 to 1.5
- value_weight: bfloat16 [8192, 1024], P('tp'), may hold values from -0.09375 to 0.09375
- queries: bfloat16 [4096, 4096], P('seq', 'tp'), may hold values from -18 to 18
- keys: bfloat16 [4096, 1024], P('seq', 'tp'), may hold values from -4.5 to 4.5
Outputs:
- mamba_out: bfloat16 [4096, 8192], P('seq', 'tp')
- attention: bfloat16 [4096, 4096], P('seq', 'tp')
All inputs are finite; a program needn't handle non-finite values.
Results may differ from a plain program's by a relative error of at most 0.02.
Values may be sent and summed in bfloat16 or wider, within the bound.
No kernel may reach another device: no remote copies, remote signals or barrier semaphores. Data moves between devices by JAX's collectives and lax.ppermute only.
A program may use at most 128 MiB of HBM per device.

v0:
```python
import math
import jax
import jax.numpy as jnp
from jax import lax
from jax.sharding import PartitionSpec as P

MHEAD_DIM = 64
STATE = 128
QHEADS = 32
KVHEADS = 8
HEAD_DIM = 128
highest = lax.Precision.HIGHEST
norm_eps = 1e-05


def carried_in(part, axis, combine, identity):
    place = lax.axis_index(axis)
    gathered = jax.tree.map(lambda a: lax.all_gather(a, axis), part)
    state = jax.tree.map(lambda a, e: jnp.zeros_like(a) + jnp.asarray(e, a.dtype), part, identity)

    def one(lap, state):
        return combine(
            state, jax.tree.map(lambda a: lax.dynamic_index_in_dim(a, lap, 0, False), gathered)
        )

    return lax.fori_loop(0, place, one, state)


def block_scan(inputs, b_group, c_group, time_step, decay_rate):
    token_count = inputs.shape[0]
    log_decay = jnp.cumsum(-time_step * decay_rate[..., None], axis=2)
    log_gaps = log_decay[..., :, None] - log_decay[..., None, :]
    causal = jnp.arange(token_count)[:, None] >= jnp.arange(token_count)[None, :]
    decay_mat = jnp.exp(jnp.where(causal, log_gaps, -jnp.inf))
    cross_terms = jnp.einsum("tgn,sgn->gts", c_group, b_group, precision=highest)
    mixing = cross_terms[:, None] * decay_mat * time_step[:, :, None, :]
    local_out = jnp.einsum("gkts,sgkp->tgkp", mixing, inputs, precision=highest)
    tail_weight = jnp.exp(log_decay[..., -1:] - log_decay) * time_step
    summary = jnp.einsum("gks,sgkp,sgn->gkpn", tail_weight, inputs, b_group, precision=highest)
    return (log_decay, local_out, summary, jnp.exp(log_decay[..., -1]))


def carried_out(c_group, state_in, log_decay):
    carried_term = jnp.einsum("tgn,gkpn->tgkp", c_group, state_in, precision=highest)
    return carried_term * jnp.transpose(jnp.exp(log_decay), (2, 0, 1))[..., None]


def gated_norm(ssm_out, gate_z, norm_gain, group_count):
    token_count = ssm_out.shape[0]
    gated = ssm_out * jax.nn.silu(gate_z.astype(jnp.float32))
    grouped = gated.reshape(token_count, group_count, -1)
    inverse = lax.rsqrt(jnp.mean(grouped * grouped, axis=2, keepdims=True) + norm_eps)
    return ((grouped * inverse).reshape(token_count, -1) * norm_gain).astype(jnp.bfloat16)


def chain_combine(earlier, latter):
    return (earlier[0] * latter[0], latter[0][..., None, None] * earlier[1] + latter[1])


def query_layout(payload, kv_here, per_kv):
    count_rows = payload.shape[0]
    shaped = payload.reshape(count_rows, kv_here, per_kv, HEAD_DIM)
    return jnp.transpose(shaped, (1, 2, 0, 3)).reshape(kv_here, per_kv * count_rows, HEAD_DIM)


def row_positions(first_pos, count_rows, per_kv):
    return jnp.tile(first_pos + jnp.arange(count_rows, dtype=jnp.int32), per_kv)


def set_output(finished_set, kv_here, per_kv):
    running_max, running_sum, running_out = finished_set
    count_rows = running_sum.shape[1] // per_kv
    result = (running_out / running_sum[..., None]).astype(jnp.bfloat16)
    result = result.reshape(kv_here, per_kv, count_rows, HEAD_DIM)
    return jnp.transpose(result, (2, 0, 1, 3)).reshape(count_rows, kv_here * per_kv * HEAD_DIM)


def attend(running, query_set, key_slab, value_slab, key_first):
    query_block, query_pos = query_set
    score_scale = 1.0 / math.sqrt(HEAD_DIM)
    key_pos = key_first + jnp.arange(key_slab.shape[1], dtype=jnp.int32)

    def update(current):
        running_max, running_sum, running_out = current
        scores = (
            jnp.einsum("hrd,hcd->hrc", query_block, key_slab, preferred_element_type=jnp.float32)
            * score_scale
        )
        allowed = key_pos[None, :] <= query_pos[:, None]
        scores = jnp.where(allowed[None], scores, -jnp.inf)
        new_max = jnp.maximum(running_max, jnp.max(scores, axis=2))
        weights = jnp.exp(scores - new_max[..., None])
        shrink = jnp.exp(running_max - new_max)
        new_sum = running_sum * shrink + jnp.sum(weights, axis=2)
        new_out = running_out * shrink[..., None] + jnp.einsum(
            "hrc,hcd->hrd",
            weights.astype(jnp.bfloat16),
            value_slab,
            preferred_element_type=jnp.float32,
        )
        return (new_max, new_sum, new_out)

    def unchanged(current):
        return current

    return lax.cond(key_first <= jnp.max(query_pos), update, unchanged, running)


def per_device(
    mamba_x, gate_z, b_in, c_in, dt_raw, a_log, skip_d, norm_gain, value_weight, queries, keys
):
    tokens_here = mamba_x.shape[0]
    group_count = b_in.shape[1] // STATE
    head_count = dt_raw.shape[0]
    per_group = head_count // group_count
    inputs = mamba_x.astype(jnp.float32).reshape(tokens_here, group_count, per_group, MHEAD_DIM)
    b_group = b_in.astype(jnp.float32).reshape(tokens_here, group_count, STATE)
    c_group = c_in.astype(jnp.float32).reshape(tokens_here, group_count, STATE)
    time_step = jax.nn.softplus(dt_raw).reshape(group_count, per_group, tokens_here)
    decay_rate = jnp.exp(a_log).reshape(group_count, per_group)
    log_decay, local_out, summary, totals = block_scan(
        inputs, b_group, c_group, time_step, decay_rate
    )
    _, state_in = carried_in(
        (totals, summary), "seq", chain_combine, (jnp.ones_like(totals), jnp.zeros_like(summary))
    )
    skip_heads = skip_d.reshape(group_count, per_group)[None, :, :, None]
    ssm_out = local_out + carried_out(c_group, state_in, log_decay) + skip_heads * inputs
    mamba_out = gated_norm(ssm_out.reshape(tokens_here, -1), gate_z, norm_gain, group_count)
    kv_here = keys.shape[1] // HEAD_DIM
    per_kv = QHEADS // KVHEADS
    product = jnp.dot(mamba_out, value_weight, preferred_element_type=jnp.float32)
    values = lax.psum_scatter(
        jnp.transpose(
            product.reshape(tokens_here, lax.axis_size("tp") * kv_here, HEAD_DIM), (1, 0, 2)
        ).astype(jnp.bfloat16),
        "tp",
        scatter_dimension=0,
        tiled=True,
    )
    key_heads = jnp.transpose(keys.reshape(tokens_here, kv_here, HEAD_DIM), (1, 0, 2))
    my_index = lax.axis_index("seq")
    query_sets = [
        (
            query_layout(queries, kv_here, per_kv),
            row_positions(my_index * tokens_here, tokens_here, per_kv),
        )
    ]
    initial = tuple(
        (
            (
                jnp.full((kv_here, query_set[0].shape[1]), -jnp.inf, jnp.float32),
                jnp.zeros((kv_here, query_set[0].shape[1]), jnp.float32),
                jnp.zeros((kv_here, query_set[0].shape[1], HEAD_DIM), jnp.float32),
            )
            for query_set in query_sets
        )
    )
    key_portion = lax.all_gather(key_heads, "seq", axis=1, tiled=True)
    value_portion = lax.all_gather(values, "seq", axis=1, tiled=True)
    length = key_portion.shape[1]
    block_len = length
    for multiple in (1, 2, 4):
        block_len = multiple * tokens_here

    def one_block(block_index, current):
        offset = block_index * block_len
        key_slab = lax.dynamic_slice_in_dim(key_portion, offset, block_len, 1)
        value_slab = lax.dynamic_slice_in_dim(value_portion, offset, block_len, 1)
        return tuple(
            (
                attend(current[set_index], query_sets[set_index], key_slab, value_slab, offset)
                for set_index in range(len(query_sets))
            )
        )

    finished = lax.fori_loop(0, length // block_len, one_block, initial)
    outputs = [set_output(finished_set, kv_here, per_kv) for finished_set in finished]
    attention = outputs[0]
    return (mamba_out, attention)


def solution(mesh):
    placed = (
        P("seq", "tp"),
        P("seq", "tp"),
        P("seq", "tp"),
        P("seq", "tp"),
        P("tp", "seq"),
        P("tp"),
        P("tp"),
        P("tp"),
        P("tp", None),
        P("seq", "tp"),
        P("seq", "tp"),
    )
    return jax.shard_map(
        per_device,
        mesh=mesh,
        in_specs=placed,
        out_specs=(P("seq", "tp"), P("seq", "tp")),
        check_vma=False,
    )
```

profile of v0, /device:TPU:480, one launch (start us, length us, event | category | flops | bytes accessed | tf_op | source)
XLA Modules:
  0.0 750.5 jit_solution(6143692668134072282)
XLA Ops:
  13.3 2.9 copy.71
  16.2 72.4 %all-gather = f32[64,16,1]{1,2,0:T(1,128)S(1)} all-gather(f32[1,16,1]{1,2,0:T(1,128)S(1)} %exp.63), channel_id=2, replica_groups=mesh['seq'=64,'tp'=8] {'seq'}, dimensions={0}, use_global_device_ids=true | all-gather | bytes 4160 | tf_op jit(solution)/shard_map/all_gather | solution.py:18
  90.2 212.9 %all-gather.9.cloned.1.call-done = f32[1024,64,128]{2,1,0:T(8,128)} async-done(((f32[16,64,128]{2,1,0:T(8,128)}), f32[1024,64,128]{2,1,0:T(8,128)}) %all-gather.9.cloned.1.call-update) | async-done | bytes 33554448 | tf_op jit(solution)/shard_map/all_gather | solution.py:18
  303.2 74.1 %while.32 = (s32[]{:T(128)}, f32[1,16,64,128]{3,2,1,0:T(8,128)S(1)}, s32[]{:T(128)}, f32[64,1,16]{2,1,0:T(1,128)S(1)}, f32[64,1,16,64,128]{4,3,2,1,0:T(8,128)}, /*index=5*/s32[]{:T(128)}, s32[]{:T(128)}, s32[]{:T(128)}) while((s32[]{:T(128)}, f32[1,16,64,128]{3,2,1,0:T(8,128)S(1)}, s32[]{:T(128)}, f32[64,1,16]{2,1,0:T(1,128)S(1)}, ...), condition=%wide.region_2.3_spmd, body=%wide.region_1.2_spmd.sunk | while | flops 262149 | bytes 1573183 | solution.py:26
  382.4 33.4 %reduce-scatter.2.cloned.1.call-done = bf16[1,64,128]{2,1,0:T(8,128)(2,1)} async-done(((bf16[8,64,128]{2,1,0:T(8,128)(2,1)}), bf16[1,64,128]{2,1,0:T(8,128)(2,1)}) %reduce-scatter.2.cloned.1.call-update) | async-done | bytes 16400 | tf_op jit(solution)/shard_map/reduce_scatter | solution.py:133
  416.7 138.2 %all-gather.11.cloned.1.call-done = bf16[4096,128]{1,0:T(8,128)(2,1)} async-done(((bf16[64,128]{1,0:T(8,128)(2,1)}), bf16[4096,128]{1,0:T(8,128)(2,1)}) %all-gather.11.cloned.1.call-update) | async-done | bytes 1048592 | tf_op jit(solution)/shard_map/all_gather | solution.py:159
  554.8 138.3 %all-gather.7.cloned.1.call-done = bf16[1,4096,128]{2,1,0:T(8,128)(2,1)} async-done(((bf16[1,64,128]{2,1,0:T(8,128)(2,1)}), bf16[1,4096,128]{2,1,0:T(8,128)(2,1)}) %all-gather.7.cloned.1.call-update) | async-done | bytes 1048592 | tf_op jit(solution)/shard_map/all_gather | solution.py:160
  693.1 50.0 %while.33 = (s32[]{:T(128)}, f32[1,256]{1,0:T(1,128)S(1)}, f32[1,256]{1,0:T(1,128)S(1)}, f32[1,256,128]{2,1,0:T(8,128)S(1)}, s32[]{:T(128)}, /*index=5*/bf16[1,4...) while((s32[]{:T(128)}, f32[1,256]{1,0:T(1,128)S(1)}, ...), condition=%wide.region_11.12_spmd.clone, body=%wide.region_6.11_spmd.clone.sunk | while | flops 34145032 | bytes 1270325 | solution.py:177
  693.8 2.4 conditional.3
  697.0 2.4 conditional.3
  700.1 2.4 conditional.3
  703.2 2.4 conditional.3
  706.3 2.4 conditional.3
  709.5 2.4 conditional.3
  712.6 2.4 conditional.3
  715.7 2.4 conditional.3
  718.8 2.4 conditional.3
  721.9 2.4 conditional.3
  725.1 2.4 conditional.3
  728.2 2.4 conditional.3
  731.3 2.4 conditional.3
  734.4 2.4 conditional.3
  737.6 2.4 conditional.3
  740.7 2.4 conditional.3
  (334 shorter events, 123.7 us)
Async XLA Ops:
  7.2 3.7 copy-start
  7.2 295.9 %all-gather.9.cloned.1.call-start = ((), (), s32[]{:S(2)}) async-start(), calls=%async_computation.3 | async-start | bytes 34078720 | tf_op jit(solution)/shard_map/all_gather | solution.py:18
  12.2 403.7 %reduce-scatter.2.cloned.1.call-start = ((), (), s32[]{:S(2)}) async-start(), calls=%async_computation.1 | async-start | bytes 147456 | tf_op jit(solution)/shard_map/reduce_scatter | solution.py:133
  13.3 75.3 %copy-start.3 = (bf16[64,128]{1,0:T(8,128)(2,1)S(1)}, bf16[64,128]{1,0:T(8,128)(2,1)}, u32[]{:S(2)}) copy-start(bf16[64,128]{1,0:T(8,128)(2,1)} %param.20) | copy-start | bytes 49156
  303.2 74.1 %copy-start.6 = (f32[16]{0:T(128)S(1)}, f32[16]{0:T(128)}, u32[]{:S(2)}) copy-start(f32[16]{0:T(128)} %param.23) | copy-start | bytes 196
  377.3 2.6 copy-start.2
  377.3 2.8 copy-start.5
  379.7 36.2 %copy-start.4 = (bf16[64,512]{1,0:T(8,128)(2,1)S(1)}, bf16[64,512]{1,0:T(8,128)(2,1)}, u32[]{:S(2)}) copy-start(bf16[64,512]{1,0:T(8,128)(2,1)} %param.26) | copy-start | bytes 196612
  380.2 312.9 %copy-start.1 = (bf16[64,1024]{1,0:T(8,128)(2,1)}, bf16[64,1024]{1,0:T(8,128)(2,1)S(1)}, u32[]{:S(2)}) copy-start(bf16[64,1024]{1,0:T(8,128)(2,1)S(1)} %multiply_convert_fusion) | copy-start | bytes 393220
  381.6 173.2 %all-gather.11.cloned.1.call-start = ((), (), s32[]{:S(2)}) async-start(), calls=%async_computation.4 | async-start | bytes 1064960 | tf_op jit(solution)/shard_map/all_gather | solution.py:159
  382.4 310.7 %all-gather.7.cloned.1.call-start = ((), (), s32[]{:S(2)}) async-start(), calls=%async_computation.2 | async-start | bytes 1064960 | tf_op jit(solution)/shard_map/all_gather | solution.py:160
Sparse Core Ops, SparseCore 0:
  12.3 290.7 all-gather.8
  381.8 34.0 reduce-scatter.1
  419.2 135.5 all-gather.10
  558.0 134.9 all-gather.6
where the time goes:
time: 755 us; the launch traced here: 750 us
  waiting for transfers between devices  523 us (69%)
  other arithmetic  75.7 us (10%)
  blocking collectives  72.4 us (10%)
  matrix products  41 us (5%)
  loops' own time  14.7 us (2%)
  between operations  14 us (2%)
  local copies, waits for them, and re-layouts  9.01 us (1%)
    all_gather x1, waiting for transfers between devices, carried_in(): gathered = jax.tree.map(lambda a: lax.all_gather(a, axis), part)  213 us
    all_gather x1, waiting for transfers between devices, per_device(): value_portion = lax.all_gather(values, 'seq', axis=1, tiled=True)  138 us
    all_gather x1, waiting for transfers between devices, per_device(): key_portion = lax.all_gather(key_heads, 'seq', axis=1, tiled=True)  138 us
    all_gather x1, blocking collectives, carried_in(): gathered = jax.tree.map(lambda a: lax.all_gather(a, axis), part)  72.4 us
    add x60, other arithmetic, chain_combine(): latter[0][..., None, None] * earlier[1] + latter[1]  71.2 us
    reduce_scatter x1, waiting for transfers between devices, per_device(): lax.psum_scatter(jnp.transpose(product.reshape(tokens_here, lax.axis_size...  33.4 us
    dot_general x16, matrix products, update(): jnp.einsum('hrc,hcd->hrd', weights.astype(jnp.bfloat16), value_slab, pref...  17.8 us
    dot_general x16, matrix products, update(): jnp.einsum('hrd,hcd->hrc', query_block, key_slab, preferred_element_type=...  17 us
  transfers between devices with their start and end apart: 4, of which 4 were waited for; matrix products, arithmetic and copies ran while one was open for 1% of the time, Pallas kernels for 0%

commit v1 on v0

--- a/solution.py
+++ b/solution.py
@@ -156,7 +156,9 @@
             for query_set in query_sets
         )
     )
-    key_portion = lax.all_gather(key_heads, "seq", axis=1, tiled=True)
+    key_portion = jnp.concatenate(
+        lax.all_to_all(jnp.stack([key_heads] * lax.axis_size("seq")), "seq", 0, 0), axis=1
+    )
     value_portion = lax.all_gather(values, "seq", axis=1, tiled=True)
     length = key_portion.shape[1]
     block_len = length

time: 755 us -> 655 us (0.87)
  waiting for transfers between devices: 523 us -> 363 us
  blocking collectives: 72.4 us -> 121 us
  starting transfers between devices: 0.16 us -> 12.5 us
    all_gather x1 -> x0, waiting for transfers between devices: 138 us -> none  [per_device(): key_portion = lax.all_gather(key_heads, 'seq', axis=1, tiled=True)]
    all_gather x1, blocking collectives: 72.4 us -> 121 us  [carried_in(): gathered = jax.tree.map(lambda a: lax.all_gather(a, axis), part)]
    all_gather x1, waiting for transfers between devices: 213 us -> 190 us  [carried_in(): gathered = jax.tree.map(lambda a: lax.all_gather(a, axis), part)]
    all_to_all x0 -> x1, starting transfers between devices: none -> 12.3 us  [per_device(): lax.all_to_all(jnp.stack([key_heads] * lax.axis_size('seq')), 'seq', 0, 0)]
  transfers between devices with their start and end apart: 4 -> 4, of which waited for: 4 -> 3; matrix products, arithmetic and copies ran while one was open for 1% -> 13% of each run, Pallas kernels for 0% -> 0%
where the time goes in v1:
time: 655 us; the launch traced here: 650 us
  waiting for transfers between devices  363 us (55%)
  blocking collectives  121 us (18%)
  other arithmetic  75.6 us (12%)
  matrix products  40.9 us (6%)
  loops' own time  14.1 us (2%)
  between operations  14 us (2%)
  starting transfers between devices  12.5 us (2%)
  local copies, waits for them, and re-layouts  10.1 us (2%)
    all_gather x1, waiting for transfers between devices, carried_in(): gathered = jax.tree.map(lambda a: lax.all_gather(a, axis), part)  190 us
    all_gather x1, waiting for transfers between devices, per_device(): value_portion = lax.all_gather(values, 'seq', axis=1, tiled=True)  138 us
    all_gather x1, blocking collectives, carried_in(): gathered = jax.tree.map(lambda a: lax.all_gather(a, axis), part)  121 us
    add x60, other arithmetic, chain_combine(): latter[0][..., None, None] * earlier[1] + latter[1]  71.2 us
    reduce_scatter x1, waiting for transfers between devices, per_device(): lax.psum_scatter(jnp.transpose(product.reshape(tokens_here, lax.axis_size...  34.2 us
    dot_general x16, matrix products, update(): jnp.einsum('hrc,hcd->hrd', weights.astype(jnp.bfloat16), value_slab, pref...  17.8 us
    dot_general x16, matrix products, update(): jnp.einsum('hrd,hcd->hrc', query_block, key_slab, preferred_element_type=...  16.9 us
  transfers between devices with their start and end apart: 4, of which 3 were waited for; matrix products, arithmetic and copies ran while one was open for 13% of the time, Pallas kernels for 0%

profile of v1, /device:TPU:480, one launch (start us, length us, event | category | flops | bytes accessed | tf_op | source)
XLA Modules:
  0.0 650.4 jit_solution(16742029486299079433)
XLA Ops:
  14.1 12.3 %all-to-all-start = ((bf16[64,1,64,128]{3,2,1,0:T(8,128)(2,1)}), bf16[64,1,64,128]{3,2,1,0:T(8,128)(2,1)}, u32[]{:S(2)}, u32[]{:S(2)}) async-start(bf16[64,1,64,128]{3,2,1,0:T(8,128)(2,1)} %stack.3), calls=%async_computation | async-start | bytes 2097152 | tf_op jit(solution)/shard_map/all_to_all | solution.py:160
  26.7 2.9 copy.71
  29.6 120.6 %all-gather = f32[64,16,1]{1,2,0:T(1,128)S(1)} all-gather(f32[1,16,1]{1,2,0:T(1,128)S(1)} %exp.63), channel_id=2, replica_groups=mesh['seq'=64,'tp'=8] {'seq'}, dimensions={0}, use_global_device_ids=true | all-gather | bytes 4160 | tf_op jit(solution)/shard_map/all_gather | solution.py:18
  151.8 190.2 %all-gather.7.cloned.1.call-done = f32[1024,64,128]{2,1,0:T(8,128)} async-done(((f32[16,64,128]{2,1,0:T(8,128)}), f32[1024,64,128]{2,1,0:T(8,128)}) %all-gather.7.cloned.1.call-update) | async-done | bytes 33554448 | tf_op jit(solution)/shard_map/all_gather | solution.py:18
  342.1 74.1 %while.32 = (s32[]{:T(128)}, f32[1,16,64,128]{3,2,1,0:T(8,128)S(1)}, s32[]{:T(128)}, f32[64,1,16]{2,1,0:T(1,128)S(1)}, f32[64,1,16,64,128]{4,3,2,1,0:T(8,128)}, /*index=5*/s32[]{:T(128)}, s32[]{:T(128)}, s32[]{:T(128)}) while((s32[]{:T(128)}, f32[1,16,64,128]{3,2,1,0:T(8,128)S(1)}, s32[]{:T(128)}, f32[64,1,16]{2,1,0:T(1,128)S(1)}, ...), condition=%wide.region_2.3_spmd, body=%wide.region_1.2_spmd.sunk | while | flops 262149 | bytes 1573183 | solution.py:26
  420.5 34.2 %reduce-scatter.2.cloned.1.call-done = bf16[1,64,128]{2,1,0:T(8,128)(2,1)} async-done(((bf16[8,64,128]{2,1,0:T(8,128)(2,1)}), bf16[1,64,128]{2,1,0:T(8,128)(2,1)}) %reduce-scatter.2.cloned.1.call-update) | async-done | bytes 16400 | tf_op jit(solution)/shard_map/reduce_scatter | solution.py:133
  455.5 138.2 %all-gather.5.cloned.1.call-done = bf16[1,4096,128]{2,1,0:T(8,128)(2,1)} async-done(((bf16[1,64,128]{2,1,0:T(8,128)(2,1)}), bf16[1,4096,128]{2,1,0:T(8,128)(2,1)}) %all-gather.5.cloned.1.call-update) | async-done | bytes 1048592 | tf_op jit(solution)/shard_map/all_gather | solution.py:162
  593.7 49.3 %while.33 = (s32[]{:T(128)}, f32[1,256]{1,0:T(1,128)S(1)}, f32[1,256]{1,0:T(1,128)S(1)}, f32[1,256,128]{2,1,0:T(8,128)S(1)}, s32[]{:T(128)}, /*index=5*/bf16[1,4...) while((s32[]{:T(128)}, f32[1,256]{1,0:T(1,128)S(1)}, ...), condition=%wide.region_11.12_spmd.clone, body=%wide.region_6.11_spmd.clone.sunk | while | flops 34145032 | bytes 1270325 | solution.py:179
  594.4 2.4 conditional.3
  597.5 2.4 conditional.3
  600.6 2.4 conditional.3
  603.6 2.4 conditional.3
  606.7 2.4 conditional.3
  609.8 2.4 conditional.3
  612.9 2.4 conditional.3
  616.0 2.4 conditional.3
  619.0 2.4 conditional.3
  622.1 2.4 conditional.3
  625.2 2.4 conditional.3
  628.3 2.4 conditional.3
  631.4 2.4 conditional.3
  634.5 2.4 conditional.3
  637.5 2.4 conditional.3
  640.6 2.4 conditional.3
  (336 shorter events, 123.9 us)
Async XLA Ops:
  7.2 3.7 copy-start
  7.2 334.8 %all-gather.7.cloned.1.call-start = ((), (), s32[]{:S(2)}) async-start(), calls=%async_computation.4 | async-start | bytes 34078720 | tf_op jit(solution)/shard_map/all_gather | solution.py:18
  10.9 15.6 %copy-start.1 = (bf16[64,1024]{1,0:T(8,128)(2,1)S(1)}, bf16[64,1024]{1,0:T(8,128)(2,1)}, u32[]{:S(2)}) copy-start(bf16[64,1024]{1,0:T(8,128)(2,1)} %param.17) | copy-start | bytes 393220
  14.1 441.3 %all-to-all-start = ((bf16[64,1,64,128]{3,2,1,0:T(8,128)(2,1)}), bf16[64,1,64,128]{3,2,1,0:T(8,128)(2,1)}, u32[]{:S(2)}, u32[]{:S(2)}) async-start(bf16[64,1,64,128]{3,2,1,0:T(8,128)(2,1)} %stack.3), calls=%async_computation | async-start | bytes 2097152 | tf_op jit(solution)/shard_map/all_to_all | solution.py:160
  26.5 428.2 %reduce-scatter.2.cloned.1.call-start = ((), (), s32[]{:S(2)}) async-start(), calls=%async_computation.2 | async-start | bytes 147456 | tf_op jit(solution)/shard_map/reduce_scatter | solution.py:133
  26.7 123.5 %copy-start.4 = (bf16[64,128]{1,0:T(8,128)(2,1)S(1)}, bf16[64,128]{1,0:T(8,128)(2,1)}, u32[]{:S(2)}) copy-start(bf16[64,128]{1,0:T(8,128)(2,1)} %param.20) | copy-start | bytes 49156
  342.0 74.1 %copy-start.7 = (f32[16]{0:T(128)S(1)}, f32[16]{0:T(128)}, u32[]{:S(2)}) copy-start(f32[16]{0:T(128)} %param.23) | copy-start | bytes 196
  416.1 2.6 copy-start.3
  416.2 2.8 copy-start.6
  418.5 36.2 %copy-start.5 = (bf16[64,512]{1,0:T(8,128)(2,1)S(1)}, bf16[64,512]{1,0:T(8,128)(2,1)}, u32[]{:S(2)}) copy-start(bf16[64,512]{1,0:T(8,128)(2,1)} %param.26) | copy-start | bytes 196612
  419.1 174.7 %copy-start.2 = (bf16[64,1024]{1,0:T(8,128)(2,1)}, bf16[64,1024]{1,0:T(8,128)(2,1)S(1)}, u32[]{:S(2)}) copy-start(bf16[64,1024]{1,0:T(8,128)(2,1)S(1)} %multiply_convert_fusion) | copy-start | bytes 393220
  420.5 173.2 %all-gather.5.cloned.1.call-start = ((), (), s32[]{:S(2)}) async-start(), calls=%async_computation.3 | async-start | bytes 1064960 | tf_op jit(solution)/shard_map/all_gather | solution.py:162
Sparse Core Ops, SparseCore 0:
  12.3 329.6 all-gather.6
  420.6 34.0 reduce-scatter.1
  458.1 135.5 all-gather.4
